TPU v7x, 512 devices: a whole 4x4x16 slice. The times are simulated.
512 devices in a mesh: par: 32 (over z, core), perp: 16 (over x, y).
Axes of the slice: x: 4, y: 4, z: 16, core: 2. Of those that a mesh axis runs over, the one named last changes fastest.
Arguments:
- fields: float32 [2, 32, 8192, 256], P(None, 'par', 'perp'), may hold values from -6 to 6
- weight_bank: float32 [8, 128, 128], replicated, may hold values from -1 to 2, as said below
- dest_slab: int32 [2, 32, 128, 1], P(None, 'par', 'perp'), may hold values from 0 to 15; in each aligned block of 8 rows (0 to 7, 8 to 15, ..., all dimensions but the last counted through in order) at most 2 rows name the same one
- dest_tile: int32 [2, 32, 128], P(None, 'par', 'perp'), may hold values from 0 to 7
- tile_blocks: int32 [2, 32, 128, 2], P(None, 'par', 'perp'), may hold values from 0 to 7
- band_terms: float32 [2, 32], replicated, may hold values from 0.45 to 0.49
Outputs:
- gradient: float32 [2, 32, 8192, 256], P(None, 'par', 'perp')
Inputs may be any that keep to these rules, and one draw needn't show every extreme that they name: `dest_slab`: in each direction and plane, at most 2 of the 8 tiles of one slab name the same destination slab, and in some slab exactly 2 do. `weight_bank`: each block is a dense real matrix.
All inputs are finite; a program needn't handle non-finite values.
Results may differ from a plain program's by a relative error of at most 0.0003.
Values sent between devices are 32-bit elements; how exact they have to be, the bound alone decides.
No kernel may reach another device: no remote copies, remote signals or barrier semaphores. Data moves between devices by JAX's collectives and lax.ppermute only.
A program may use at most 64 MiB of HBM per device.

v0:
```python
import jax
import jax.numpy as jnp
from jax import lax
from jax.sharding import PartitionSpec as P

TILE = 128
PRECISE = lax.Precision.HIGHEST
KAPPA = 0.125


def extended(block, sides, width):
    for axis, dim in sides:
        count = lax.axis_size(axis)
        forward = [(i, i + 1) for i in range(count - 1)]
        backward = [(target, source) for source, target in forward]
        low = lax.ppermute(
            lax.slice_in_dim(block, block.shape[dim] - width, None, axis=dim), axis, forward
        )
        high = lax.ppermute(lax.slice_in_dim(block, 0, width, axis=dim), axis, backward)
        block = jnp.concatenate([low, block, high], axis=dim)
    return block


def split_tiles(plane_pair):
    field_count, row_count, col_count = plane_pair.shape
    shaped = plane_pair.reshape(field_count, row_count // TILE, TILE, col_count // TILE, TILE)
    return shaped.transpose(0, 1, 3, 2, 4).reshape(field_count, -1, TILE, TILE)


def join_tiles(tile_set, row_count, col_count):
    field_count = tile_set.shape[0]
    shaped = tile_set.reshape(field_count, row_count // TILE, col_count // TILE, TILE, TILE)
    return shaped.transpose(0, 1, 3, 2, 4).reshape(field_count, row_count, col_count)


def coefficients(band_terms):
    plane_total = band_terms.shape[1]
    lower, pivots, ratios = ([], [], [])
    previous = jnp.zeros((), jnp.float32)
    for p in range(plane_total):
        lower_now = band_terms[0, p] if p > 0 else jnp.zeros((), jnp.float32)
        upper_now = band_terms[1, p] if p < plane_total - 1 else jnp.zeros((), jnp.float32)
        pivot_now = 1.0 - lower_now * previous
        ratio_now = upper_now / pivot_now
        lower.append(lower_now)
        pivots.append(pivot_now)
        ratios.append(ratio_now)
        previous = ratio_now
    return (lower, pivots, ratios)


def slot_labels(dest_slabs, target, peer_count, capacity):
    tile_count = dest_slabs.shape[-1]
    position = jnp.arange(tile_count, dtype=jnp.int32)
    earlier = position[:, None] > position[None, :]
    shared = dest_slabs[..., :, None] == dest_slabs[..., None, :]
    slot_rank = jnp.sum((shared & earlier).astype(jnp.int32), axis=-1)
    peer_ids = jnp.arange(peer_count, dtype=jnp.int32)
    slot_ids = jnp.arange(capacity, dtype=jnp.int32)
    chosen = (dest_slabs[..., None, None, :] == peer_ids[:, None, None]) & (
        slot_rank[..., None, None, :] == slot_ids[None, :, None]
    )
    return chosen


def local(fields, weight_bank, dest_slab, dest_tile, tile_blocks, band_terms):
    peer_count = lax.axis_size("perp")
    plane_count = lax.axis_size("par")
    row_count = fields.shape[2]
    col_count = fields.shape[3]
    local_pair = fields[:, 0]
    tile_set = split_tiles(local_pair)
    tile_count = tile_set.shape[1]
    capacity = max(2, (tile_count + peer_count - 1) // peer_count)
    dest_slabs = dest_slab[:, 0, :, 0]
    target = dest_tile[:, 0, :]
    left_index = tile_blocks[:, 0, :, 0]
    right_index = tile_blocks[:, 0, :, 1]
    left_block = jnp.take(weight_bank, left_index, axis=0, mode="clip")
    right_block = jnp.take(weight_bank, right_index, axis=0, mode="clip")
    shifted = jnp.einsum("dsij,dsjk->dsik", left_block, tile_set, precision=PRECISE)
    moved = jnp.einsum("dsik,dslk->dsil", shifted, right_block, precision=PRECISE)
    chosen = slot_labels(dest_slabs, target, peer_count, capacity)
    picker = chosen.astype(jnp.float32)
    packed = jnp.einsum("dpcs,dsij->dpcij", picker, moved, precision=PRECISE)
    moved_tiles = lax.all_to_all(packed, "perp", split_axis=1, concat_axis=1, tiled=True)
    all_slabs = lax.all_gather(dest_slabs, "perp", axis=1, tiled=True)
    all_targets = lax.all_gather(target, "perp", axis=1, tiled=True)
    field_count = all_slabs.shape[0]
    all_slabs = all_slabs.reshape(field_count, peer_count, tile_count)
    all_targets = all_targets.reshape(field_count, peer_count, tile_count)
    source_chosen = slot_labels(all_slabs, all_targets, peer_count, capacity)
    me = lax.axis_index("perp")
    mine = source_chosen[:, :, me]
    arrived_target = jnp.sum(mine.astype(jnp.int32) * (all_targets[:, :, None, :] + 1), axis=-1) - 1
    position = jnp.arange(tile_count, dtype=jnp.int32)
    flattened = moved_tiles.reshape(field_count, peer_count * capacity, TILE, TILE)
    flat_target = arrived_target.reshape(field_count, peer_count * capacity)
    landing = (flat_target[:, None, :] == position[None, :, None]).astype(jnp.float32)
    summed = jnp.einsum("dts,dsij->dtij", landing, flattened, precision=PRECISE)
    deposit = join_tiles(summed, row_count, col_count)
    upward = [(i, i + 1) for i in range(plane_count - 1)]
    downward = [(i + 1, i) for i in range(plane_count - 1)]
    mapped = jnp.stack(
        (lax.ppermute(deposit[0], "par", upward), lax.ppermute(deposit[1], "par", downward))
    )
    rimmed = extended(mapped, (("perp", 1),), 1)
    padded = jnp.pad(rimmed, ((0, 0), (0, 0), (1, 1)))
    beside_all = (
        padded[:, 2:, 1:-1] + padded[:, :-2, 1:-1] + padded[:, 1:-1, 2:] + padded[:, 1:-1, :-2]
    )
    smoothed = mapped + KAPPA * (beside_all - 4.0 * mapped)
    orient = jnp.array([1.0, -1.0], jnp.float32)[:, None, None]
    right_side = orient * (local_pair - smoothed)
    lower, pivots, ratios = coefficients(band_terms)
    column_block = lax.all_to_all(
        right_side[:, None], "par", split_axis=2, concat_axis=1, tiled=True
    )
    depth_count = column_block.shape[1]
    eliminated = []
    previous = None
    for p in range(depth_count):
        current = column_block[:, p]
        if previous is not None:
            current = current - lower[p] * previous
        current = current / pivots[p]
        eliminated.append(current)
        previous = current
    solved = [None] * depth_count
    following = None
    for p in reversed(range(depth_count)):
        current = eliminated[p]
        if following is not None:
            current = current - ratios[p] * following
        solved[p] = current
        following = current
    solved = jnp.stack(solved, axis=1)
    result = lax.all_to_all(solved, "par", split_axis=1, concat_axis=2, tiled=True)
    return result


def solution(mesh):
    placed = (
        P(None, "par", "perp", None),
        P(),
        P(None, "par", "perp", None),
        P(None, "par", "perp"),
        P(None, "par", "perp", None),
        P(),
    )
    return jax.shard_map(
        local, mesh=mesh, in_specs=placed, out_specs=P(None, "par", "perp", None), check_vma=False
    )
```

profile of v0, /device:TPU:4, one launch (start us, length us, event | category | flops | bytes accessed | tf_op | source)
XLA Modules:
  0.0 324.2 jit_solution(12230348033059756992)
XLA Ops:
  0.0 0.8 slice_reduce_fusion
  1.0 1.7 reshape_squeeze.3
  2.8 0.6 gather_fusion
  3.5 1.6 gather_fusion.1
  5.4 1.2 fusion.71
  6.5 2.3 convolution_bitcast_fusion
  8.8 2.1 fusion.7
  10.9 3.2 %copy.173 = f32[2,16,2,128,128]{4,3,2,0,1:T(8,128)} copy(f32[2,16,2,128,128]{4,1,3,2,0:T(8,128)S(1)} %fusion.7) | data formatting | bytes 8388608 | tf_op jit(solution)/shard_map/dpcs,dsij->dpcij/dot_general | solution.py:85
  14.2 10.3 %all-to-all-start = ((f32[2,16,2,128,128]{4,3,2,0,1:T(8,128)}), f32[2,16,2,128,128]{4,3,2,0,1:T(8,128)}, u32[]{:S(2)}, u32[]{:S(2)}) async-start(f32[2,16,2,128,128]{4,3,2,0,1:T(8,128)} %copy.173), calls=%async_computation | async-start | bytes 8388608 | tf_op jit(solution)/shard_map/all_to_all | solution.py:86
  24.6 62.2 %all-gather.1 = s32[2,1,128]{0,1,2:T(1,128)S(1)} all-gather(s32[2,1,8]{0,1,2:T(1,128)S(1)} %copy.167), channel_id=3, replica_groups=mesh['par'=32,'perp'=16] {'perp'}, dimensions={2}, use_global_device_ids=true | all-gather | bytes 1088 | tf_op jit(solution)/shard_map/all_gather | solution.py:88
  87.1 23.7 %all-gather = s32[2,1,128,1]{0,3,1,2:T(1,128)S(1)} all-gather(s32[2,1,8,1]{0,3,1,2:T(1,128)S(1)} %copy.162), channel_id=2, replica_groups=mesh['par'=32,'perp'=16] {'perp'}, dimensions={2}, use_global_device_ids=true | all-gather | bytes 1088 | tf_op jit(solution)/shard_map/all_gather | solution.py:87
  111.3 2.5 copy.174
  113.8 3.9 %fusion = f32[2,8,128,128]{3,1,2,0:T(8,128)S(1)} fusion(f32[2,32,128,128]{3,2,1,0:T(8,128)S(1)} %bitcast.114, s32[2,32]{1,0:T(2,128)S(1)} %sub.1780), kind=kOutput, calls=%fused_computation.2 | convolution fusion | flops 100663808 | bytes 5243136 | tf_op jit(solution)/shard_map/dts,dsij->dtij/dot_general | solution.py:100
  118.2 1.3 collective-permute-start
  119.8 1.3 collective-permute-start.1
  121.5 17.7 %collective-permute-done.1 = f32[512,256]{1,0:T(8,128)S(1)} collective-permute-done((f32[512,256]{1,0:T(8,128)S(1)}, f32[512,256]{1,0:T(8,128)S(1)}, u32[]{:S(2)}, u32[]{:S(2)}) %collective-permute-start.1) | collective-permute-done | bytes 524320 | tf_op jit(solution)/shard_map/ppermute | solution.py:105
  139.5 4.1 %collective-permute-start.2 = (f32[2,1,256]{2,0,1:T(2,128)S(1)}, f32[2,1,256]{2,0,1:T(2,128)S(1)}, u32[]{:S(2)}, u32[]{:S(2)}) collective-permute-start(f32[2,1,256]{2,0,1:T(2,128)S(1)} %get-tuple-element.71), channel_id=1, source_target_pairs={{1,0},{2,1},{3,2},{4,3},{5,4},{6,5},{7,6},{8,7},{9,8},{10,9},{11,1... | collective-permute-start | bytes 6152 | tf_op jit(solution)/shard_map/ppermute | solution.py:19
  143.7 1.9 collective-permute-start.3
  145.6 5.6 %collective-permute-done.3 = f32[2,1,256]{2,0,1:T(2,128)S(1)} collective-permute-done((f32[2,1,256]{2,0,1:T(2,128)S(1)}, f32[2,1,256]{2,0,1:T(2,128)S(1)}, u32[]{:S(2)}, u32[]{:S(2)}) %collective-permute-start.3) | collective-permute-done | bytes 2080 | tf_op jit(solution)/shard_map/ppermute | solution.py:16
  151.2 5.3 %select_maximum_fusion = f32[2,514,258]{2,0,1:T(2,128)S(1)} fusion(f32[2,1,256]{2,0,1:T(2,128)S(1)} %collective-permute-done.2, f32[2,1,256]{2,0,1:T(2,128)S(1)} %collective-permute-done.3, f32[1,512,256]{2,0,1:T(1,128)S(1)} %stack.9, f32[1,512,256]{2,0,1:T(1,128)S(1)} %stack.8), kind=kLoop, calls=%fused_computation.5 | loop fusion | flops 2652240 | bytes 2113568 | tf_op jit(solution)/shard_map/concatenate | solution.py:20
  156.5 6.2 %multiply_bitcast_fusion = f32[2,1,512,256]{3,0,1,2:T(2,128)} fusion(f32[2,514,258]{2,0,1:T(2,128)S(1)} %select_maximum_fusion, f32[1,512,256]{2,0,1:T(1,128)S(1)} %stack.9, f32[1,512,256]{2,0,1:T(1,128)S(1)} %stack.8, f32[2,1,256]{2,0,1:T(2,128)S(1)} %collective-permute-done.3, f32[2,1,256]{2,0,1:T(2,128)S(1)} %collective-permute-done.2, ...), kind=kLoop, calls=%fused_computation.27 | loop fusion | flops 3670016 | bytes 5246984 | tf_op jit(solution)/shard_map/broadcast_in_dim | solution.py:117
  162.7 22.1 %all-to-all-start.1 = ((f32[2,1,512,256]{3,0,1,2:T(2,128)}), f32[2,1,512,256]{3,0,1,2:T(2,128)S(1)}, u32[]{:S(2)}, u32[]{:S(2)}) async-start(f32[2,1,512,256]{3,0,1,2:T(2,128)} %multiply_bitcast_fusion), calls=%async_computation.1 | async-start | bytes 2097152 | tf_op jit(solution)/shard_map/all_to_all | solution.py:116
  184.9 0.7 fusion.70
  188.6 0.7 fusion.69
  200.8 0.7 fusion.68
  212.9 0.7 fusion.67
  226.6 14.0 %all-to-all-done.1 = f32[2,1,512,256]{3,0,1,2:T(2,128)S(1)} async-done(((f32[2,1,512,256]{3,0,1,2:T(2,128)}), f32[2,1,512,256]{3,0,1,2:T(2,128)S(1)}, u32[]{:S(2)}, u32[]{:S(2)}) %all-to-all-start.1) | async-done | bytes 1048608 | tf_op jit(solution)/shard_map/all_to_all | solution.py:116
  241.1 20.9 %constant_dynamic-update-slice_fusion.31 = (f32[2,32,16,256]{3,2,0,1:T(8,128)S(1)}, f32[2,1,16,256]{3,2,0,1:T(8,128)S(1)}, f32[2,1,16,256]{3,2,0,1:T(8,128)S(1)}...) fusion(f32[2,1,16,256]{3,0,2,1:T(2,128)S(1)} %get-tuple-element, ...), kind=kLoop, calls=%fused_computation.62 | loop fusion | flops 1269759 | bytes 2064756
  262.4 0.6 constant_dynamic-update-slice_fusion.1
  263.1 0.6 constant_dynamic-update-slice_fusion
  263.7 59.5 %all_to_all.29 = f32[2,32,16,256]{3,2,0,1:T(8,128)S(1)} all-to-all(f32[2,32,16,256]{3,2,0,1:T(8,128)S(1)} %constant_dynamic-update-slice_fusion), channel_id=1, replica_groups=mesh['par'=32,'perp'=16] {'par'}, dimensions={1} | all-to-all | bytes 2097152 | tf_op jit(solution)/shard_map/all_to_all | solution.py:138
  323.2 1.1 copy.210
  (79 shorter events, 3.6 us)
Async XLA Ops:
  0.0 2.8 copy-start
  2.8 2.2 copy-start.4
  5.1 1.4 copy-start.1
  14.2 10.4 %copy-start.5 = (s32[2,1,8]{2,1,0:T(1,128)S(1)}, s32[2,1,8]{2,1,0:T(1,128)}, u32[]{:S(2)}) copy-start(s32[2,1,8]{2,1,0:T(1,128)} %param.10) | copy-start | bytes 196
  14.2 97.1 %all-to-all-start = ((f32[2,16,2,128,128]{4,3,2,0,1:T(8,128)}), f32[2,16,2,128,128]{4,3,2,0,1:T(8,128)}, u32[]{:S(2)}, u32[]{:S(2)}) async-start(f32[2,16,2,128,128]{4,3,2,0,1:T(8,128)} %copy.173), calls=%async_computation | async-start | bytes 8388608 | tf_op jit(solution)/shard_map/all_to_all | solution.py:86
  118.2 2.9 collective-permute-start
  119.8 19.3 %collective-permute-start.1 = (f32[512,256]{1,0:T(8,128)S(1)}, f32[512,256]{1,0:T(8,128)S(1)}, u32[]{:S(2)}, u32[]{:S(2)}) collective-permute-start(f32[512,256]{1,0:T(8,128)S(1)} %bitcast.125), channel_id=1, source_target_pairs={{16,0},{32,16},{48,32},{64,48},{80,64},{96,80},{112,96},{128,112},... | collective-permute-start | bytes 1572872 | tf_op jit(solution)/shard_map/ppermute | solution.py:105
  139.5 17.0 %copy-start.2 = (f32[2,1,512,256]{3,2,1,0:T(8,128)S(1)}, f32[2,1,512,256]{3,2,1,0:T(8,128)}, u32[]{:S(2)}) copy-start(f32[2,1,512,256]{3,2,1,0:T(8,128)} %param.7) | copy-start | bytes 3145732
  139.5 17.0 %copy-start.6 = (f32[2]{0:T(128)S(1)}, f32[2]{0:T(128)}, u32[]{:S(2)}) copy-start(f32[2]{0:T(128)} %constant.25.clone) | copy-start | bytes 28
  139.5 6.0 %collective-permute-start.2 = (f32[2,1,256]{2,0,1:T(2,128)S(1)}, f32[2,1,256]{2,0,1:T(2,128)S(1)}, u32[]{:S(2)}, u32[]{:S(2)}) collective-permute-start(f32[2,1,256]{2,0,1:T(2,128)S(1)} %get-tuple-element.71), channel_id=1, source_target_pairs={{1,0},{2,1},{3,2},{4,3},{5,4},{6,5},{7,6},{8,7},{9,8},{10,9},{11,1... | collective-permute-start | bytes 6152 | tf_op jit(solution)/shard_map/ppermute | solution.py:19
  143.7 7.6 %collective-permute-start.3 = (f32[2,1,256]{2,0,1:T(2,128)S(1)}, f32[2,1,256]{2,0,1:T(2,128)S(1)}, u32[]{:S(2)}, u32[]{:S(2)}) collective-permute-start(f32[2,1,256]{2,0,1:T(2,128)S(1)} %get-tuple-element.70), channel_id=1, source_target_pairs={{0,1},{1,2},{2,3},{3,4},{4,5},{5,6},{6,7},{7,8},{8,9},{9,10},{10,1... | collective-permute-start | bytes 6152 | tf_op jit(solution)/shard_map/ppermute | solution.py:16
  162.7 22.1 %copy-start.3 = (f32[2,32]{1,0:T(2,128)S(1)}, f32[2,32]{1,0:T(2,128)}, u32[]{:S(2)}) copy-start(f32[2,32]{1,0:T(2,128)} %param.12) | copy-start | bytes 772
  162.7 77.9 %all-to-all-start.1 = ((f32[2,1,512,256]{3,0,1,2:T(2,128)}), f32[2,1,512,256]{3,0,1,2:T(2,128)S(1)}, u32[]{:S(2)}, u32[]{:S(2)}) async-start(f32[2,1,512,256]{3,0,1,2:T(2,128)} %multiply_bitcast_fusion), calls=%async_computation.1 | async-start | bytes 2097152 | tf_op jit(solution)/shard_map/all_to_all | solution.py:116
where the time goes:
time: 326 us; the launch traced here: 324 us
  blocking collectives  145 us (44%)
  starting transfers between devices  41.1 us (13%)
  between operations  39.5 us (12%)
  waiting for transfers between devices  37.3 us (11%)
  other arithmetic  34.2 us (10%)
  local copies, waits for them, and re-layouts  17.3 us (5%)
  matrix products  9.36 us (3%)
    all_gather x1, blocking collectives, local(): all_targets = lax.all_gather(target, 'perp', axis=1, tiled=True)  62.2 us
    all_to_all x1, blocking collectives, local(): lax.all_to_all(solved, 'par', split_axis=1, concat_axis=2, tiled=True)  59.5 us
    all_gather x1, blocking collectives, local(): all_slabs = lax.all_gather(dest_slabs, 'perp', axis=1, tiled=True)  23.7 us
    all_to_all x1, starting transfers between devices, local(): lax.all_to_all(right_side[:, None], 'par', split_axis=2, concat_axis=1, t...  22.1 us
    unnamed x16, other arithmetic  21.7 us
    ppermute x1, waiting for transfers between devices, local(): lax.ppermute(deposit[1], 'par', downward)  17.7 us
    all_to_all x1, waiting for transfers between devices, local(): lax.all_to_all(right_side[:, None], 'par', split_axis=2, concat_axis=1, t...  14 us
    all_to_all x1, starting transfers between devices, local(): lax.all_to_all(packed, 'perp', split_axis=1, concat_axis=1, tiled=True)  10.3 us
  transfers between devices with their start and end apart: 6, of which 3 were waited for; matrix products, arithmetic and copies ran while one was open for 1% of the time, Pallas kernels for 0%

commit v1 on v0

--- a/solution.py
+++ b/solution.py
@@ -85,7 +85,10 @@
     packed = jnp.einsum("dpcs,dsij->dpcij", picker, moved, precision=PRECISE)
     moved_tiles = lax.all_to_all(packed, "perp", split_axis=1, concat_axis=1, tiled=True)
     all_slabs = lax.all_gather(dest_slabs, "perp", axis=1, tiled=True)
-    all_targets = lax.all_gather(target, "perp", axis=1, tiled=True)
+    all_targets = jnp.concatenate(
+        lax.all_to_all(jnp.stack([target for _ in range(lax.axis_size("perp"))]), "perp", 0, 0),
+        axis=1,
+    )
     field_count = all_slabs.shape[0]
     all_slabs = all_slabs.reshape(field_count, peer_count, tile_count)
     all_targets = all_targets.reshape(field_count, peer_count, tile_count)

time: 326 us -> 304 us (0.933)
  the two profiles are of different devices: /device:TPU:4 before, /device:TPU:2 now
where the time goes in v1:
time: 304 us; the launch traced here: 302 us
  blocking collectives  123 us (40%)
  starting transfers between devices  47.2 us (16%)
  between operations  39.5 us (13%)
  other arithmetic  34.3 us (11%)
  waiting for transfers between devices  30.6 us (10%)
  local copies, waits for them, and re-layouts  18.4 us (6%)
  matrix products  9.38 us (3%)
    all_gather x1, blocking collectives, local(): all_slabs = lax.all_gather(dest_slabs, 'perp', axis=1, tiled=True)  63.6 us
    all_to_all x1, blocking collectives, local(): lax.all_to_all(solved, 'par', split_axis=1, concat_axis=2, tiled=True)  59.5 us
    all_to_all x1, starting transfers between devices, local(): lax.all_to_all(right_side[:, None], 'par', split_axis=2, concat_axis=1, t...  22.1 us
    unnamed x16, other arithmetic  21.7 us
    all_to_all x1, waiting for transfers between devices, local(): lax.all_to_all(right_side[:, None], 'par', split_axis=2, concat_axis=1, t...  14 us
    ppermute x1, waiting for transfers between devices, local(): lax.ppermute(deposit[1], 'par', downward)  11.8 us
    all_to_all x1, starting transfers between devices, local(): lax.all_to_all(jnp.stack([target for _ in range(lax.axis_size('perp'))]),...  9.18 us
    all_to_all x1, starting transfers between devices, local(): lax.all_to_all(packed, 'perp', split_axis=1, concat_axis=1, tiled=True)  7.26 us
  transfers between devices with their start and end apart: 7, of which 3 were waited for; matrix products, arithmetic and copies ran while one was open for 6% of the time, Pallas kernels for 0%

profile of v1, /device:TPU:2, one launch (start us, length us, event | category | flops | bytes accessed | tf_op | source)
XLA Modules:
  0.0 302.4 jit_solution(6735869032401068307)
XLA Ops:
  0.0 1.3 stack.10
  1.3 9.2 %all-to-all-start = ((s32[16,2,8]{2,1,0:T(2,128)}), s32[16,2,8]{2,1,0:T(2,128)S(1)}, u32[]{:S(2)}, u32[]{:S(2)}) async-start(s32[16,2,8]{2,1,0:T(2,128)} %stack.10), calls=%async_computation | async-start | bytes 32768 | tf_op jit(solution)/shard_map/all_to_all | solution.py:89
  10.5 0.8 slice_reduce_fusion
  11.5 1.7 reshape_squeeze.3
  14.0 1.6 gather_fusion.1
  15.9 1.2 fusion.71
  17.0 2.3 convolution_bitcast_fusion
  19.3 2.1 fusion.7
  21.4 3.2 %copy.118 = f32[2,16,2,128,128]{4,3,2,0,1:T(8,128)} copy(f32[2,16,2,128,128]{4,1,3,2,0:T(8,128)S(1)} %fusion.7) | data formatting | bytes 8388608 | tf_op jit(solution)/shard_map/dpcs,dsij->dpcij/dot_general | solution.py:85
  24.7 7.3 %all-to-all-start.1 = ((f32[2,16,2,128,128]{4,3,2,0,1:T(8,128)}), f32[2,16,2,128,128]{4,3,2,0,1:T(8,128)}, u32[]{:S(2)}, u32[]{:S(2)}) async-start(f32[2,16,2,128,128]{4,3,2,0,1:T(8,128)} %copy.118), calls=%async_computation.1 | async-start | bytes 8388608 | tf_op jit(solution)/shard_map/all_to_all | solution.py:86
  32.0 63.6 %all-gather = s32[2,1,128,1]{0,3,1,2:T(1,128)S(1)} all-gather(s32[2,1,8,1]{0,3,1,2:T(1,128)S(1)} %copy.109), channel_id=2, replica_groups=mesh['par'=32,'perp'=16] {'perp'}, dimensions={2}, use_global_device_ids=true | all-gather | bytes 1088 | tf_op jit(solution)/shard_map/all_gather | solution.py:87
  96.2 2.5 copy.119
  98.7 3.9 %fusion = f32[2,8,128,128]{3,1,2,0:T(8,128)S(1)} fusion(f32[2,32,128,128]{3,2,1,0:T(8,128)S(1)} %bitcast.115, s32[2,32]{1,0:T(2,128)S(1)} %sub.1780), kind=kOutput, calls=%fused_computation.2 | convolution fusion | flops 100663808 | bytes 5243136 | tf_op jit(solution)/shard_map/dts,dsij->dtij/dot_general | solution.py:103
  103.1 1.3 collective-permute-start
  104.7 1.3 collective-permute-start.1
  106.3 11.8 %collective-permute-done.1 = f32[512,256]{1,0:T(8,128)S(1)} collective-permute-done((f32[512,256]{1,0:T(8,128)S(1)}, f32[512,256]{1,0:T(8,128)S(1)}, u32[]{:S(2)}, u32[]{:S(2)}) %collective-permute-start.1) | collective-permute-done | bytes 524320 | tf_op jit(solution)/shard_map/ppermute | solution.py:108
  118.5 3.2 %collective-permute-start.2 = (f32[2,1,256]{2,0,1:T(2,128)S(1)}, f32[2,1,256]{2,0,1:T(2,128)S(1)}, u32[]{:S(2)}, u32[]{:S(2)}) collective-permute-start(f32[2,1,256]{2,0,1:T(2,128)S(1)} %get-tuple-element.71), channel_id=1, source_target_pairs={{1,0},{2,1},{3,2},{4,3},{5,4},{6,5},{7,6},{8,7},{9,8},{10,9},{11,1... | collective-permute-start | bytes 6152 | tf_op jit(solution)/shard_map/ppermute | solution.py:19
  121.7 2.8 collective-permute-start.3
  124.5 4.8 %collective-permute-done.3 = f32[2,1,256]{2,0,1:T(2,128)S(1)} collective-permute-done((f32[2,1,256]{2,0,1:T(2,128)S(1)}, f32[2,1,256]{2,0,1:T(2,128)S(1)}, u32[]{:S(2)}, u32[]{:S(2)}) %collective-permute-start.3) | collective-permute-done | bytes 2080 | tf_op jit(solution)/shard_map/ppermute | solution.py:16
  129.3 5.3 %select_maximum_fusion = f32[2,514,258]{2,0,1:T(2,128)S(1)} fusion(f32[2,1,256]{2,0,1:T(2,128)S(1)} %collective-permute-done.2, f32[2,1,256]{2,0,1:T(2,128)S(1)} %collective-permute-done.3, f32[1,512,256]{2,0,1:T(1,128)S(1)} %stack.12, f32[1,512,256]{2,0,1:T(1,128)S(1)} %stack.11), kind=kLoop, calls=%fused_computation.5 | loop fusion | flops 2652240 | bytes 2113568 | tf_op jit(solution)/shard_map/concatenate | solution.py:20
  134.6 6.2 %multiply_bitcast_fusion = f32[2,1,512,256]{3,0,1,2:T(2,128)} fusion(f32[2,514,258]{2,0,1:T(2,128)S(1)} %select_maximum_fusion, f32[1,512,256]{2,0,1:T(1,128)S(1)} %stack.12, f32[1,512,256]{2,0,1:T(1,128)S(1)} %stack.11, f32[2,1,256]{2,0,1:T(2,128)S(1)} %collective-permute-done.3, f32[2,1,256]{2,0,1:T(2,128)S(1)} %collective-permute-done.2, ...), kind=kLoop, calls=%fused_computation.27 | loop fusion | flops 3670016 | bytes 5246984 | tf_op jit(solution)/shard_map/broadcast_in_dim | solution.py:120
  140.8 22.1 %all-to-all-start.2 = ((f32[2,1,512,256]{3,0,1,2:T(2,128)}), f32[2,1,512,256]{3,0,1,2:T(2,128)S(1)}, u32[]{:S(2)}, u32[]{:S(2)}) async-start(f32[2,1,512,256]{3,0,1,2:T(2,128)} %multiply_bitcast_fusion), calls=%async_computation.2 | async-start | bytes 2097152 | tf_op jit(solution)/shard_map/all_to_all | solution.py:119
  163.0 0.7 fusion.70
  166.7 0.7 fusion.69
  178.9 0.7 fusion.68
  191.0 0.7 fusion.67
  204.7 14.0 %all-to-all-done.2 = f32[2,1,512,256]{3,0,1,2:T(2,128)S(1)} async-done(((f32[2,1,512,256]{3,0,1,2:T(2,128)}), f32[2,1,512,256]{3,0,1,2:T(2,128)S(1)}, u32[]{:S(2)}, u32[]{:S(2)}) %all-to-all-start.2) | async-done | bytes 1048608 | tf_op jit(solution)/shard_map/all_to_all | solution.py:119
  219.1 20.9 %constant_dynamic-update-slice_fusion.31 = (f32[2,32,16,256]{3,2,0,1:T(8,128)S(1)}, f32[2,1,16,256]{3,2,0,1:T(8,128)S(1)}, f32[2,1,16,256]{3,2,0,1:T(8,128)S(1)}...) fusion(f32[2,1,16,256]{3,0,2,1:T(2,128)S(1)} %get-tuple-element, ...), kind=kLoop, calls=%fused_computation.62 | loop fusion | flops 1269759 | bytes 2064756
  240.5 0.6 constant_dynamic-update-slice_fusion.1
  241.2 0.6 constant_dynamic-update-slice_fusion
  241.8 59.5 %all_to_all.34 = f32[2,32,16,256]{3,2,0,1:T(8,128)S(1)} all-to-all(f32[2,32,16,256]{3,2,0,1:T(8,128)S(1)} %constant_dynamic-update-slice_fusion), channel_id=1, replica_groups=mesh['par'=32,'perp'=16] {'par'}, dimensions={1} | all-to-all | bytes 2097152 | tf_op jit(solution)/shard_map/all_to_all | solution.py:141
  301.3 1.1 copy.155
  (76 shorter events, 4.0 us)
Async XLA Ops:
  0.0 13.3 %copy-start = (f32[8,128,128]{2,1,0:T(8,128)S(1)}, f32[8,128,128]{2,1,0:T(8,128)}, u32[]{:S(2)}) copy-start(f32[8,128,128]{2,1,0:T(8,128)} %param.8) | copy-start | bytes 1572868
  1.3 23.3 %all-to-all-start = ((s32[16,2,8]{2,1,0:T(2,128)}), s32[16,2,8]{2,1,0:T(2,128)S(1)}, u32[]{:S(2)}, u32[]{:S(2)}) async-start(s32[16,2,8]{2,1,0:T(2,128)} %stack.10), calls=%async_computation | async-start | bytes 32768 | tf_op jit(solution)/shard_map/all_to_all | solution.py:89
  13.4 2.2 copy-start.4
  15.7 1.4 copy-start.1
  24.7 71.5 %all-to-all-start.1 = ((f32[2,16,2,128,128]{4,3,2,0,1:T(8,128)}), f32[2,16,2,128,128]{4,3,2,0,1:T(8,128)}, u32[]{:S(2)}, u32[]{:S(2)}) async-start(f32[2,16,2,128,128]{4,3,2,0,1:T(8,128)} %copy.118), calls=%async_computation.1 | async-start | bytes 8388608 | tf_op jit(solution)/shard_map/all_to_all | solution.py:86
  103.1 2.9 collective-permute-start
  104.7 13.4 %collective-permute-start.1 = (f32[512,256]{1,0:T(8,128)S(1)}, f32[512,256]{1,0:T(8,128)S(1)}, u32[]{:S(2)}, u32[]{:S(2)}) collective-permute-start(f32[512,256]{1,0:T(8,128)S(1)} %bitcast.126), channel_id=1, source_target_pairs={{16,0},{32,16},{48,32},{64,48},{80,64},{96,80},{112,96},{128,112},... | collective-permute-start | bytes 1572872 | tf_op jit(solution)/shard_map/ppermute | solution.py:108
  118.5 16.1 %copy-start.2 = (f32[2,1,512,256]{3,2,1,0:T(8,128)S(1)}, f32[2,1,512,256]{3,2,1,0:T(8,128)}, u32[]{:S(2)}) copy-start(f32[2,1,512,256]{3,2,1,0:T(8,128)} %param.7) | copy-start | bytes 3145732
  118.5 16.1 %copy-start.5 = (f32[2]{0:T(128)S(1)}, f32[2]{0:T(128)}, u32[]{:S(2)}) copy-start(f32[2]{0:T(128)} %constant.25.clone) | copy-start | bytes 28
  118.5 6.0 %collective-permute-start.2 = (f32[2,1,256]{2,0,1:T(2,128)S(1)}, f32[2,1,256]{2,0,1:T(2,128)S(1)}, u32[]{:S(2)}, u32[]{:S(2)}) collective-permute-start(f32[2,1,256]{2,0,1:T(2,128)S(1)} %get-tuple-element.71), channel_id=1, source_target_pairs={{1,0},{2,1},{3,2},{4,3},{5,4},{6,5},{7,6},{8,7},{9,8},{10,9},{11,1... | collective-permute-start | bytes 6152 | tf_op jit(solution)/shard_map/ppermute | solution.py:19
  121.7 7.6 %collective-permute-start.3 = (f32[2,1,256]{2,0,1:T(2,128)S(1)}, f32[2,1,256]{2,0,1:T(2,128)S(1)}, u32[]{:S(2)}, u32[]{:S(2)}) collective-permute-start(f32[2,1,256]{2,0,1:T(2,128)S(1)} %get-tuple-element.70), channel_id=1, source_target_pairs={{0,1},{1,2},{2,3},{3,4},{4,5},{5,6},{6,7},{7,8},{8,9},{9,10},{10,1... | collective-permute-start | bytes 6152 | tf_op jit(solution)/shard_map/ppermute | solution.py:16
  140.8 22.2 %copy-start.3 = (f32[2,32]{1,0:T(2,128)S(1)}, f32[2,32]{1,0:T(2,128)}, u32[]{:S(2)}) copy-start(f32[2,32]{1,0:T(2,128)} %param.12) | copy-start | bytes 772
  140.8 77.9 %all-to-all-start.2 = ((f32[2,1,512,256]{3,0,1,2:T(2,128)}), f32[2,1,512,256]{3,0,1,2:T(2,128)S(1)}, u32[]{:S(2)}, u32[]{:S(2)}) async-start(f32[2,1,512,256]{3,0,1,2:T(2,128)} %multiply_bitcast_fusion), calls=%async_computation.2 | async-start | bytes 2097152 | tf_op jit(solution)/shard_map/all_to_all | solution.py:119
